TPU v7x, 32 devices: a whole 2x2x4 slice. The times are simulated.
32 devices in a mesh: axial: 8 (over y, x, core), radial: 4 (over z).
Axes of the slice: x: 2, y: 2, z: 4, core: 2. Of those that a mesh axis runs over, the one named last changes fastest.
Arguments:
- composition_deviations: float32 [38, 1024, 512], P(None, 'axial', 'radial'), may hold values from -6 to 6
- flow_speed_vector: float32 [2, 1024, 512], P(None, 'axial', 'radial'), may hold values from -1 to 1
- thermal_field: float32 [1024, 512], P('axial', 'radial'), may hold values from 0.4 to 4
- linearized_kinetics_operator: float32 [38, 38], replicated, may hold values from -0.5 to 0.5
- frozen_jacobian_inverse_addend: float32 [38, 38], replicated, may hold values from -0.25 to 0.25
- rigid_block_indicator: int32 [512, 4], P('axial', 'radial'), may hold values from 0 to 1, as said below
- molar_absorptivity_table: float32 [4, 38], replicated, may hold values from -1 to 1
- spokewise_sightline_length: float32 [512], P('radial'), may hold values from 0.3 to 3
- sightline_lengthwise_index: int32 [4, 32768], replicated, may hold values from 0 to 1023
- observed_absorbance_traces: float32 [4, 32768], P(None, ('axial', 'radial')), may hold values from -6 to 6
Outputs:
- species_out: float32 [38, 1024, 512], P(None, 'axial', 'radial')
- misfit: float32 [4, 32768], P(None, ('axial', 'radial'))
Inputs may be any that keep to these rules, and one draw needn't show every extreme that they name: `rigid_block_indicator`: in each radial column of tiles, the tiles of 2 cyclically consecutive axial devices are all stiff and every other axial device holds exactly 8 stiff tiles, so the column holds 176 stiff tiles.
All inputs are finite; a program needn't handle non-finite values.
Results may differ from a plain program's by a relative error of at most 0.0001.
Values sent between devices are 32-bit elements; how exact they have to be, the bound alone decides.
No kernel may reach another device: no remote copies, remote signals or barrier semaphores. Data moves between devices by JAX's collectives and lax.ppermute only.
A program may use at most 192 MiB of HBM per device.

v0:
```python
import math
import jax
import jax.numpy as jnp
from jax import lax
from jax.sharding import PartitionSpec as P

TILE_ROWS = 2
ITERS = 3
TIME_STEP = 0.4
CHEM_STEP = 0.5
ARRHENIUS_BARRIER = 1.0
WENO_EPS = 1e-06
HIGHEST = lax.Precision.HIGHEST


def extended(shard, sides, width):
    for axis, dim in sides:
        peers, length = (lax.axis_size(axis), shard.shape[dim])
        up = [(i, (i + 1) % peers) for i in range(peers - 1)]
        down = [(j, i) for i, j in up]
        last = lax.slice_in_dim(shard, length - width, length, axis=dim)
        initial = lax.slice_in_dim(shard, 0, width, axis=dim)
        before = lax.ppermute(last, axis, up)
        after = lax.ppermute(initial, axis, down)
        shard = jnp.concatenate([before, shard, after], axis=dim)
    return shard


def weno_side(minus_two, minus_one, centre, plus_one, plus_two):
    beta_zero = (
        13.0 / 12.0 * (minus_two - 2.0 * minus_one + centre) ** 2
        + 0.25 * (minus_two - 4.0 * minus_one + 3.0 * centre) ** 2
    )
    beta_one = (
        13.0 / 12.0 * (minus_one - 2.0 * centre + plus_one) ** 2
        + 0.25 * (minus_one - plus_one) ** 2
    )
    beta_two = (
        13.0 / 12.0 * (centre - 2.0 * plus_one + plus_two) ** 2
        + 0.25 * (3.0 * centre - 4.0 * plus_one + plus_two) ** 2
    )
    weight_zero = 0.1 / (WENO_EPS + beta_zero) ** 2
    weight_one = 0.6 / (WENO_EPS + beta_one) ** 2
    weight_two = 0.3 / (WENO_EPS + beta_two) ** 2
    weight_total = weight_zero + weight_one + weight_two
    blended = weight_zero * (2.0 * minus_two - 7.0 * minus_one + 11.0 * centre)
    blended = blended + weight_one * (-minus_one + 5.0 * centre + 2.0 * plus_one)
    blended = blended + weight_two * (2.0 * centre + 5.0 * plus_one - plus_two)
    return blended / (6.0 * weight_total)


def face_difference(field, speed, along, length):
    face_count = length + 1

    def cut_part(offset):
        return lax.slice_in_dim(field, offset, offset + face_count, axis=along)

    left_value = weno_side(cut_part(0), cut_part(1), cut_part(2), cut_part(3), cut_part(4))
    right_value = weno_side(cut_part(5), cut_part(4), cut_part(3), cut_part(2), cut_part(1))
    face_speed = 0.5 * (
        lax.slice_in_dim(speed, 2, 2 + face_count, axis=along)
        + lax.slice_in_dim(speed, 3, 3 + face_count, axis=along)
    )
    face_flux = (
        jnp.maximum(face_speed, 0.0) * left_value + jnp.minimum(face_speed, 0.0) * right_value
    )
    return lax.slice_in_dim(face_flux, 1, face_count, axis=along) - lax.slice_in_dim(
        face_flux, 0, face_count - 1, axis=along
    )


def transport(field_pad, speed_pad):
    row_count = field_pad.shape[1] - 6
    col_count = field_pad.shape[2] - 6
    along_axial = face_difference(field_pad[:, :, 3:-3], speed_pad[0:1, :, 3:-3], 1, row_count)
    along_radial = face_difference(field_pad[:, 3:-3, :], speed_pad[1:2, 3:-3, :], 2, col_count)
    return field_pad[:, 3:-3, 3:-3] - TIME_STEP * (along_axial + along_radial)


def kinetics_advance(
    starting_composition_field,
    thermal_field,
    linearized_kinetics_operator,
    frozen_jacobian_inverse_addend,
):
    acceleration_factor = jnp.exp(-ARRHENIUS_BARRIER / thermal_field)
    current = starting_composition_field
    for newton_step in range(ITERS):
        source = jnp.tensordot(
            linearized_kinetics_operator, current, axes=(1, 0), precision=HIGHEST
        ) - jnp.tanh(current)
        defect = current - starting_composition_field - CHEM_STEP * acceleration_factor * source
        current = (
            current
            - defect
            - jnp.tensordot(frozen_jacobian_inverse_addend, defect, axes=(1, 0), precision=HIGHEST)
        )
    return current


def absorbance_profile(field, molar_absorptivity_table, spokewise_sightline_length):
    mixed = jnp.tensordot(molar_absorptivity_table, field, axes=(1, 0), precision=HIGHEST)
    return jnp.dot(mixed, spokewise_sightline_length, precision=HIGHEST)


def local(
    composition_deviations,
    flow_speed_vector,
    thermal_field,
    linearized_kinetics_operator,
    frozen_jacobian_inverse_addend,
    rigid_block_indicator,
    molar_absorptivity_table,
    spokewise_sightline_length,
    sightline_lengthwise_index,
    observed_absorbance_traces,
):
    species_count = composition_deviations.shape[0]
    stacked = jnp.concatenate([composition_deviations, flow_speed_vector], axis=0)
    padded = extended(stacked, (("axial", 1), ("radial", 2)), 3)
    advected_composition_field = transport(padded[:species_count], padded[species_count:])
    combusted_composition_field = kinetics_advance(
        advected_composition_field,
        thermal_field,
        linearized_kinetics_operator,
        frozen_jacobian_inverse_addend,
    )
    flag_cells = jnp.repeat(
        jnp.repeat(rigid_block_indicator, TILE_ROWS, axis=0),
        advected_composition_field.shape[2],
        axis=1,
    )
    species_out = jnp.where(
        flag_cells[None] > 0, combusted_composition_field, advected_composition_field
    )
    path_scale = 1.0 / math.sqrt(advected_composition_field.shape[2] * lax.axis_size("radial"))
    profile = (
        absorbance_profile(species_out, molar_absorptivity_table, spokewise_sightline_length)
        * path_scale
    )
    column = lax.psum(profile, "radial")
    whole_profile = lax.all_gather(column, "axial", axis=1, tiled=True)
    device = lax.axis_index(("axial", "radial"))
    sample_count = observed_absorbance_traces.shape[1]
    own_rows = lax.dynamic_slice_in_dim(
        sightline_lengthwise_index, device * sample_count, sample_count, 1
    )
    values = jnp.take_along_axis(whole_profile, own_rows, axis=1)
    return (species_out, values - observed_absorbance_traces)


def solution(mesh):
    in_specs = (
        P(None, "axial", "radial"),
        P(None, "axial", "radial"),
        P("axial", "radial"),
        P(),
        P(),
        P("axial", "radial"),
        P(),
        P("radial"),
        P(),
        P(None, ("axial", "radial")),
    )
    out_specs = (P(None, "axial", "radial"), P(None, ("axial", "radial")))
    return jax.shard_map(local, mesh=mesh, in_specs=in_specs, out_specs=out_specs, check_vma=False)
```

profile of v0, /device:TPU:0, one launch (start us, length us, event | category | flops | bytes accessed | tf_op | source)
XLA Modules:
  0.0 168.7 jit_solution(240044641915545838)
XLA Ops:
  0.7 2.6 %copy.75 = f32[38,128,128]{1,0,2:T(8,128)S(1)} copy(f32[38,128,128]{2,1,0:T(8,128)} %param.10) | data formatting | bytes 4980736 | tf_op args[0]
  3.4 3.3 %slice_maximum_fusion = (f32[40,3,128]{1,0,2:T(8,128)}, f32[40,3,128]{1,0,2:T(8,128)}) fusion(f32[2,128,128]{1,0,2:T(2,128)S(1)} %copy.64, f32[38,128,128]{1,0,2:T(8,128)S(1)} %copy.75), kind=kLoop, calls=%fused_computation.63 | loop fusion | flops 30720 | bytes 2744320 | tf_op jit(solution)/shard_map/concatenate | solution.py:119
  6.7 2.5 %copy.67 = f32[40,3,128]{2,0,1:T(8,128)S(1)} copy(f32[40,3,128]{1,0,2:T(8,128)} %get-tuple-element.25) | data formatting | bytes 122880 | tf_op jit(solution)/shard_map/slice | solution.py:22
  10.5 2.5 %copy.65 = f32[40,3,128]{2,0,1:T(8,128)S(1)} copy(f32[40,3,128]{1,0,2:T(8,128)} %get-tuple-element.24) | data formatting | bytes 122880 | tf_op jit(solution)/shard_map/slice | solution.py:21
  13.1 3.0 %collective-permute-start = (f32[40,3,128]{2,0,1:T(8,128)S(1)}, f32[40,3,128]{2,0,1:T(8,128)S(1)}, u32[]{:S(2)}, u32[]{:S(2)}) collective-permute-start(f32[40,3,128]{2,0,1:T(8,128)S(1)} %copy.65), channel_id=1, source_target_pairs={{0,4},{4,8},{8,12},{12,16},{16,20},{20,24},{24,28},{1,5},{5,9},{9,... | collective-permute-start | bytes 184328 | tf_op jit(solution)/shard_map/ppermute | solution.py:23
  17.3 2.3 %copy.68 = f32[40,3,128]{1,0,2:T(8,128)} copy(f32[40,3,128]{2,0,1:T(8,128)S(1)} %collective-permute-done.1) | data formatting | bytes 122880 | tf_op jit(solution)/shard_map/ppermute | solution.py:24
  19.6 2.3 %copy.66 = f32[40,3,128]{1,0,2:T(8,128)} copy(f32[40,3,128]{2,0,1:T(8,128)S(1)} %collective-permute-done) | data formatting | bytes 122880 | tf_op jit(solution)/shard_map/ppermute | solution.py:23
  24.5 2.7 %maximum_maximum_fusion.1 = (f32[40,131,128]{1,0,2:T(8,128)S(1)}, f32[40,131,128]{1,0,2:T(8,128)S(1)}) fusion(f32[2,128,128]{1,0,2:T(2,128)S(1)} %copy.64, f32[38,128,128]{1,0,2:T(8,128)S(1)} %copy.75, f32[40,3,128]{1,0,2:T(8,128)S(1)} %copy-done.2, f32[40,3,128]{1,0,2:T(8,128)S(1)} %copy-done.1), kind=kLoop, calls=%fused_computation.3 | loop fusion | flops 2682880 | bytes 8110080 | tf_op jit(solution)/shard_map/concatenate | solution.py:25
  28.0 4.9 %collective-permute-start.2 = (f32[40,134,3]{1,0,2:T(8,128)S(1)}, f32[40,134,3]{1,0,2:T(8,128)S(1)}, u32[]{:S(2)}, u32[]{:S(2)}) collective-permute-start(f32[40,134,3]{1,0,2:T(8,128)S(1)} %get-tuple-element.20), channel_id=1, source_target_pairs={{0,1},{1,2},{2,3},{4,5},{5,6},{6,7},{8,9},{9,10},{10,11},{12,13},{... | collective-permute-start | bytes 192968 | tf_op jit(solution)/shard_map/ppermute | solution.py:23
  34.5 25.3 %multiply_add_fusion = f32[38,129,128]{1,0,2:T(8,128)} fusion(f32[40,131,128]{1,0,2:T(8,128)S(1)} %get-tuple-element.23, f32[40,131,128]{1,0,2:T(8,128)S(1)} %get-tuple-element.22, f32[129,128]{0,1:T(8,128)S(1)} %get-tuple-element.28, f32[129,128]{0,1:T(8,128)S(1)} %get-tuple-element.29), kind=kLoop, calls=%fused_computation.5 | loop fusion | flops 77177088 | bytes 17700864 | tf_op jit(solution)/shard_map/add | solution.py:65
  60.2 7.2 %maximum_maximum_fusion = (f32[40,134,131]{1,0,2:T(8,128)S(1)}, f32[40,134,131]{1,0,2:T(8,128)S(1)}) fusion(f32[40,3,128]{1,0,2:T(8,128)S(1)} %copy-done.1, f32[2,128,128]{1,0,2:T(2,128)S(1)} %copy.64, f32[38,128,128]{1,0,2:T(8,128)S(1)} %copy.75, f32[40,3,128]{1,0,2:T(8,128)S(1)} %copy-done.2, f32[40,134,3]{1,0,2:T(8,128)S(1)} %collective-permute-done.2, ...), kind=kLoop, calls=%fused_computation.1 | loop fusion | flops 5617280 | bytes 8490240 | tf_op jit(solution)/shard_map/concatenate | solution.py:25
  67.4 13.0 %multiply_add_fusion.3 = f32[38,128,129]{1,0,2:T(8,128)S(1)} fusion(f32[40,134,131]{1,0,2:T(8,128)S(1)} %get-tuple-element.19, f32[40,134,131]{1,0,2:T(8,128)S(1)} %get-tuple-element.18, f32[128,129]{0,1:T(8,128)S(1)} %get-tuple-element.26, f32[128,129]{0,1:T(8,128)S(1)} %get-tuple-element.27), kind=kLoop, calls=%fused_computation.31 | loop fusion | flops 77177088 | bytes 17700864 | tf_op jit(solution)/shard_map/add | solution.py:65
  80.5 4.3 %fusion.44 = f32[38,128,128]{1,0,2:T(8,128)S(1)} fusion(f32[38,128,128]{1,0,2:T(8,128)S(1)} %copy.75, f32[38,128,129]{1,0,2:T(8,128)S(1)} %multiply_add_fusion.3, f32[38,129,128]{1,0,2:T(8,128)} %multiply_add_fusion), kind=kLoop, calls=%fused_computation.60 | loop fusion | flops 3112960 | bytes 14942208 | tf_op jit(solution)/shard_map/sub | solution.py:77
  84.8 2.5 %fusion.78 = f32[128,128,38]{0,2,1:T(8,128)S(1)} fusion(f32[38,128,128]{1,0,2:T(8,128)S(1)} %fusion.44, f32[38,38]{1,0:T(8,128)S(1)} %copy-done), kind=kOutput, calls=%fused_computation.113 | convolution fusion | flops 283901952 | bytes 4986512 | tf_op jit(solution)/shard_map/dot_general | solution.py:89
  87.3 4.1 %bitcast_subtract_fusion.4 = f32[38,128,128]{1,0,2:T(8,128)S(1)} fusion(f32[38,128,128]{1,0,2:T(8,128)S(1)} %fusion.44, f32[128,128,38]{0,2,1:T(8,128)S(1)} %fusion.78, f32[128,128]{0,1:T(8,128)S(1)} %copy.76, f32[38,38]{1,0:T(8,128)S(1)} %copy-done.4), kind=kOutput, calls=%fused_computation.73 | convolution fusion | flops 290127872 | bytes 7542416 | tf_op jit(solution)/shard_map/dot_general | solution.py:96
  91.4 2.4 %fusion.76 = f32[128,128,38]{0,2,1:T(8,128)S(1)} fusion(f32[38,128,128]{1,0,2:T(8,128)S(1)} %bitcast_subtract_fusion.4, f32[38,38]{1,0:T(8,128)S(1)} %copy-done), kind=kOutput, calls=%fused_computation.111 | convolution fusion | flops 283901952 | bytes 4986512 | tf_op jit(solution)/shard_map/dot_general | solution.py:89
  93.8 4.5 %bitcast_subtract_fusion.2 = f32[38,128,128]{1,0,2:T(8,128)S(1)} fusion(f32[38,128,128]{1,0,2:T(8,128)S(1)} %bitcast_subtract_fusion.4, f32[128,128,38]{0,2,1:T(8,128)S(1)} %fusion.76, f32[38,128,128]{1,0,2:T(8,128)S(1)} %fusion.44, f32[128,128]{0,1:T(8,128)S(1)} %copy.76, f32[38,38]{1,0:T(8,128)S(1)} %copy-done.4), kind=kOutput, calls=%fused_computation.69 | convolution fusion | flops 290127872 | bytes 10032784 | tf_op jit(solution)/shard_map/dot_general | solution.py:96
  98.3 2.3 %fusion.74 = f32[128,128,38]{0,2,1:T(8,128)S(1)} fusion(f32[38,128,128]{1,0,2:T(8,128)S(1)} %bitcast_subtract_fusion.2, f32[38,38]{1,0:T(8,128)S(1)} %copy-done), kind=kOutput, calls=%fused_computation.109 | convolution fusion | flops 283901952 | bytes 4986512 | tf_op jit(solution)/shard_map/dot_general | solution.py:89
  100.6 4.4 %fusion.45 = f32[38,128,128]{1,0,2:T(8,128)S(1)} fusion(f32[38,128,128]{1,0,2:T(8,128)S(1)} %fusion.44, f32[38,128,128]{1,0,2:T(8,128)S(1)} %bitcast_subtract_fusion.2, f32[128,128,38]{0,2,1:T(8,128)S(1)} %fusion.74, f32[128,128]{0,1:T(8,128)S(1)} %copy.76, pred[128]{0:T(512)(128)(4,1)S(1)} %gt.22, f32[38,38]{1,0:T(8,128)S(1)} %copy-done.4), kind=kOutput, calls=%fused_computation.65 | convolution fusion | flops 290750464 | bytes 10032912 | tf_op jit(solution)/shard_map/dot_general | solution.py:96
  104.9 2.1 %copy.77 = f32[38,128,128]{2,1,0:T(8,128)} copy(f32[38,128,128]{1,0,2:T(8,128)S(1)} %fusion.45) | data formatting | bytes 4980736
  107.1 1.7 %convolution_bitcast_fusion = f32[4,128,128]{1,0,2:T(4,128)S(1)} fusion(f32[38,128,128]{1,0,2:T(8,128)S(1)} %fusion.45, f32[4,38]{1,0:T(4,128)S(1)} %copy-done.7), kind=kOutput, calls=%fused_computation.85 | convolution fusion | flops 29884416 | bytes 2753120 | tf_op jit(solution)/shard_map/dot_general | solution.py:102
  109.1 13.0 %psum.7 = f32[4,128]{1,0:T(4,128)S(1)} all-reduce(f32[4,128]{1,0:T(4,128)S(1)} %broadcast_multiply_fusion), channel_id=1, replica_groups=mesh['axial'=8,'radial'=4] {'radial'}, use_global_device_ids=true, to_apply=%region_0.1 | all-reduce | flops 512 | bytes 4096 | tf_op jit(solution)/shard_map/psum | solution.py:141
  122.1 10.3 %all_gather.3 = f32[4,1024]{1,0:T(4,128)S(1)} all-gather(f32[4,128]{1,0:T(4,128)S(1)} %psum.7), channel_id=1, replica_groups=mesh['axial'=8,'radial'=4] {'axial'}, dimensions={1}, use_global_device_ids=true | all-gather | bytes 18432 | tf_op jit(solution)/shard_map/all_gather | solution.py:142
  132.4 35.0 %gather_fusion = f32[4096]{0:T(1024)S(1)} fusion(f32[4,1024]{1,0:T(4,128)S(1)} %all_gather.3, s32[4096]{0:T(1024)S(1)} %bitcast.92), kind=kCustom, calls=%fused_computation | custom fusion | bytes 65536 | tf_op jit(solution)/shard_map/jit(take_along_axis)/gather | solution.py:148
  (45 shorter events, 9.6 us)
Async XLA Ops:
  0.6 84.1 %copy-start = (f32[38,38]{1,0:T(8,128)S(1)}, f32[38,38]{1,0:T(8,128)}, u32[]{:S(2)}) copy-start(f32[38,38]{1,0:T(8,128)} %param.13) | copy-start | bytes 17332
  0.6 2.6 %copy-start.3 = (f32[2,128,128]{2,1,0:T(8,128)S(1)}, f32[2,128,128]{2,1,0:T(8,128)}, u32[]{:S(2)}) copy-start(f32[2,128,128]{2,1,0:T(8,128)} %param.11) | copy-start | bytes 393220
  6.7 9.4 %copy-start.5 = (f32[128,128]{1,0:T(8,128)S(1)}, f32[128,128]{1,0:T(8,128)}, u32[]{:S(2)}) copy-start(f32[128,128]{1,0:T(8,128)} %param.12) | copy-start | bytes 196612
  6.7 9.6 %copy-start.9 = (s32[64,1]{0,1:T(1,128)S(1)}, s32[64,1]{0,1:T(1,128)}, u32[]{:S(2)}) copy-start(s32[64,1]{0,1:T(1,128)} %param.15) | copy-start | bytes 772
  9.2 8.0 %collective-permute-start.1 = (f32[40,3,128]{2,0,1:T(8,128)S(1)}, f32[40,3,128]{2,0,1:T(8,128)S(1)}, u32[]{:S(2)}, u32[]{:S(2)}) collective-permute-start(f32[40,3,128]{2,0,1:T(8,128)S(1)} %copy.67), channel_id=1, source_target_pairs={{4,0},{8,4},{12,8},{16,12},{20,16},{24,20},{28,24},{5,1},{9,5},{13... | collective-permute-start | bytes 184328 | tf_op jit(solution)/shard_map/ppermute | solution.py:24
  13.1 6.5 %collective-permute-start = (f32[40,3,128]{2,0,1:T(8,128)S(1)}, f32[40,3,128]{2,0,1:T(8,128)S(1)}, u32[]{:S(2)}, u32[]{:S(2)}) collective-permute-start(f32[40,3,128]{2,0,1:T(8,128)S(1)} %copy.65), channel_id=1, source_target_pairs={{0,4},{4,8},{8,12},{12,16},{16,20},{20,24},{24,28},{1,5},{5,9},{9,... | collective-permute-start | bytes 184328 | tf_op jit(solution)/shard_map/ppermute | solution.py:23
  21.9 1.9 %copy-start.1 = (f32[40,3,128]{1,0,2:T(8,128)S(1)}, f32[40,3,128]{1,0,2:T(8,128)}, u32[]{:S(2)}) copy-start(f32[40,3,128]{1,0,2:T(8,128)} %copy.68) | copy-start | bytes 184324
  21.9 2.6 %copy-start.2 = (f32[40,3,128]{1,0,2:T(8,128)S(1)}, f32[40,3,128]{1,0,2:T(8,128)}, u32[]{:S(2)}) copy-start(f32[40,3,128]{1,0,2:T(8,128)} %copy.66) | copy-start | bytes 184324
  28.0 31.9 %collective-permute-start.2 = (f32[40,134,3]{1,0,2:T(8,128)S(1)}, f32[40,134,3]{1,0,2:T(8,128)S(1)}, u32[]{:S(2)}, u32[]{:S(2)}) collective-permute-start(f32[40,134,3]{1,0,2:T(8,128)S(1)} %get-tuple-element.20), channel_id=1, source_target_pairs={{0,1},{1,2},{2,3},{4,5},{5,6},{6,7},{8,9},{9,10},{10,11},{12,13},{... | collective-permute-start | bytes 192968 | tf_op jit(solution)/shard_map/ppermute | solution.py:23
  32.9 26.9 %collective-permute-start.3 = (f32[40,134,3]{1,0,2:T(8,128)S(1)}, f32[40,134,3]{1,0,2:T(8,128)S(1)}, u32[]{:S(2)}, u32[]{:S(2)}) collective-permute-start(f32[40,134,3]{1,0,2:T(8,128)S(1)} %get-tuple-element.21), channel_id=1, source_target_pairs={{1,0},{2,1},{3,2},{5,4},{6,5},{7,6},{9,8},{10,9},{11,10},{13,12},{... | collective-permute-start | bytes 192968 | tf_op jit(solution)/shard_map/ppermute | solution.py:24
  84.8 2.5 %copy-start.4 = (f32[38,38]{1,0:T(8,128)S(1)}, f32[38,38]{1,0:T(8,128)}, u32[]{:S(2)}) copy-start(f32[38,38]{1,0:T(8,128)} %param.14) | copy-start | bytes 17332
  104.9 2.1 %copy-start.7 = (f32[4,38]{1,0:T(4,128)S(1)}, f32[4,38]{1,0:T(4,128)}, u32[]{:S(2)}) copy-start(f32[4,38]{1,0:T(4,128)} %param.16) | copy-start | bytes 1828
  107.1 1.7 %copy-start.8 = (f32[128]{0:T(128)S(1)}, f32[128]{0:T(128)}, u32[]{:S(2)}) copy-start(f32[128]{0:T(128)} %param.17) | copy-start | bytes 1540
  132.4 35.0 %copy-start.6 = (f32[4,1024]{1,0:T(4,128)S(1)}, f32[4,1024]{1,0:T(4,128)}, u32[]{:S(2)}) copy-start(f32[4,1024]{1,0:T(4,128)} %param.19) | copy-start | bytes 49156
where the time goes:
time: 169 us
  other arithmetic  60.4 us (36%)
  local copies, waits for them, and re-layouts  51.3 us (30%)
  blocking collectives  23.3 us (14%)
  matrix products  22.1 us (13%)
  starting transfers between devices  10.7 us (6%)
    add x2, other arithmetic, face_difference(): jnp.maximum(face_speed, 0.0) * left_value  38.3 us
    gather x2, local copies, waits for them, and re-layouts, local(): values = jnp.take_along_axis(whole_profile, own_rows, axis=1)  35 us
    psum x1, blocking collectives, local(): column = lax.psum(profile, 'radial')  13 us
    dot_general x3, matrix products, kinetics_advance(): jnp.tensordot(frozen_jacobian_inverse_addend, defect, axes=(1, 0), precis...  13 us
    all_gather x1, blocking collectives, local(): whole_profile = lax.all_gather(column, 'axial', axis=1, tiled=True)  10.3 us
    concatenate x2, other arithmetic, extended(): shard = jnp.concatenate([before, shard, after], axis=dim)  9.84 us
    ppermute x2, starting transfers between devices, extended(): before = lax.ppermute(last, axis, up)  7.97 us
    dot_general x3, matrix products, kinetics_advance(): jnp.tensordot(linearized_kinetics_operator, current, axes=(1, 0), precisi...  7.12 us
  transfers between devices with their start and end apart: 4, of which 0 were waited for; matrix products, arithmetic and copies ran while one was open for 19% of the time, Pallas kernels for 0%

commit v1 on v0

--- a/solution.py
+++ b/solution.py
@@ -11,6 +11,27 @@
 ARRHENIUS_BARRIER = 1.0
 WENO_EPS = 1e-06
 HIGHEST = lax.Precision.HIGHEST
+
+
+def gather_around(array, axis, dim):
+    count, index, span = (lax.axis_size(axis), lax.axis_index(axis), array.shape[dim])
+    upward = [(i, (i + 1) % count) for i in range(count)]
+    downward = [(i, (i - 1) % count) for i in range(count)]
+    result = jnp.zeros((*array.shape[:dim], count * span, *array.shape[dim + 1 :]), array.dtype)
+    result = lax.dynamic_update_slice_in_dim(result, array, index * span, axis=dim)
+    from_left = from_right = array
+    halfway = count // 2
+    for hop in range(1, halfway + 1):
+        from_left = lax.ppermute(from_left, axis, upward)
+        result = lax.dynamic_update_slice_in_dim(
+            result, from_left, (index - hop) % count * span, axis=dim
+        )
+        if hop < count - halfway:
+            from_right = lax.ppermute(from_right, axis, downward)
+            result = lax.dynamic_update_slice_in_dim(
+                result, from_right, (index + hop) % count * span, axis=dim
+            )
+    return result
 
 
 def extended(shard, sides, width):
@@ -139,7 +160,7 @@
         * path_scale
     )
     column = lax.psum(profile, "radial")
-    whole_profile = lax.all_gather(column, "axial", axis=1, tiled=True)
+    whole_profile = gather_around(column, "axial", 1)
     device = lax.axis_index(("axial", "radial"))
     sample_count = observed_absorbance_traces.shape[1]
     own_rows = lax.dynamic_slice_in_dim(

time: 169 us -> 175 us (1.036)
  blocking collectives: 23.3 us -> 13 us
  starting transfers between devices: 10.7 us -> 18.6 us
  waiting for transfers between devices: 0.01 us -> 6.44 us
    all_gather x1 -> x0, blocking collectives: 10.3 us -> none  [local(): whole_profile = lax.all_gather(column, 'axial', axis=1, tiled=True)]
    ppermute x0 -> x7, starting transfers between devices: none -> 7.91 us  [the longest x3 7.86 us: gather_around(): from_right = lax.ppermute(from_right, axis, downward)]
    ppermute x0 -> x7, waiting for transfers between devices: none -> 6.43 us  [the longest x4 6.34 us: gather_around(): from_left = lax.ppermute(from_left, axis, upward)]
    unnamed x25 -> x27, local copies, waits for them, and re-layouts: 6.29 us -> 7.51 us
  transfers between devices with their start and end apart: 4 -> 11, of which waited for: 0 -> 3; matrix products, arithmetic and copies ran while one was open for 19% -> 20% of each run, Pallas kernels for 0% -> 0%
where the time goes in v1:
time: 175 us
  other arithmetic  60.4 us (35%)
  local copies, waits for them, and re-layouts  52.6 us (30%)
  matrix products  22.3 us (13%)
  starting transfers between devices  18.6 us (11%)
  blocking collectives  13 us (7%)
  waiting for transfers between devices  6.44 us (4%)
    add x2, other arithmetic, face_difference(): jnp.maximum(face_speed, 0.0) * left_value  38.3 us
    gather x2, local copies, waits for them, and re-layouts, local(): values = jnp.take_along_axis(whole_profile, own_rows, axis=1)  35 us
    dot_general x3, matrix products, kinetics_advance(): jnp.tensordot(frozen_jacobian_inverse_addend, defect, axes=(1, 0), precis...  13.1 us
    psum x1, blocking collectives, local(): column = lax.psum(profile, 'radial')  13 us
    concatenate x2, other arithmetic, extended(): shard = jnp.concatenate([before, shard, after], axis=dim)  9.84 us
    ppermute x2, starting transfers between devices, extended(): before = lax.ppermute(last, axis, up)  7.97 us
    ppermute x3, starting transfers between devices, gather_around(): from_right = lax.ppermute(from_right, axis, downward)  7.86 us
    unnamed x27, local copies, waits for them, and re-layouts  7.51 us
  transfers between devices with their start and end apart: 11, of which 3 were waited for; matrix products, arithmetic and copies ran while one was open for 20% of the time, Pallas kernels for 0%

profile of v1, /device:TPU:0, one launch (start us, length us, event | category | flops | bytes accessed | tf_op | source)
XLA Modules:
  0.0 174.6 jit_solution(18335846069664959861)
XLA Ops:
  0.7 2.6 %copy.75 = f32[38,128,128]{1,0,2:T(8,128)S(1)} copy(f32[38,128,128]{2,1,0:T(8,128)} %param.10) | data formatting | bytes 4980736 | tf_op args[0]
  3.4 3.3 %slice_maximum_fusion = (f32[40,3,128]{1,0,2:T(8,128)}, f32[40,3,128]{1,0,2:T(8,128)}) fusion(f32[2,128,128]{1,0,2:T(2,128)S(1)} %copy.64, f32[38,128,128]{1,0,2:T(8,128)S(1)} %copy.75), kind=kLoop, calls=%fused_computation.63 | loop fusion | flops 30720 | bytes 2744320 | tf_op jit(solution)/shard_map/concatenate | solution.py:140
  6.7 2.5 %copy.67 = f32[40,3,128]{2,0,1:T(8,128)S(1)} copy(f32[40,3,128]{1,0,2:T(8,128)} %get-tuple-element.25) | data formatting | bytes 122880 | tf_op jit(solution)/shard_map/slice | solution.py:43
  10.6 2.5 %copy.65 = f32[40,3,128]{2,0,1:T(8,128)S(1)} copy(f32[40,3,128]{1,0,2:T(8,128)} %get-tuple-element.24) | data formatting | bytes 122880 | tf_op jit(solution)/shard_map/slice | solution.py:42
  13.1 3.0 %collective-permute-start = (f32[40,3,128]{2,0,1:T(8,128)S(1)}, f32[40,3,128]{2,0,1:T(8,128)S(1)}, u32[]{:S(2)}, u32[]{:S(2)}) collective-permute-start(f32[40,3,128]{2,0,1:T(8,128)S(1)} %copy.65), channel_id=1, source_target_pairs={{0,4},{4,8},{8,12},{12,16},{16,20},{20,24},{24,28},{1,5},{5,9},{9,... | collective-permute-start | bytes 184328 | tf_op jit(solution)/shard_map/ppermute | solution.py:44
  24.8 2.7 %maximum_maximum_fusion.1 = (f32[40,131,128]{1,0,2:T(8,128)S(1)}, f32[40,131,128]{1,0,2:T(8,128)S(1)}) fusion(f32[2,128,128]{1,0,2:T(2,128)S(1)} %copy.64, f32[38,128,128]{1,0,2:T(8,128)S(1)} %copy.75, f32[40,3,128]{1,0,2:T(8,128)S(1)} %copy-done.2, f32[40,3,128]{1,0,2:T(8,128)S(1)} %copy-done.1), kind=kLoop, calls=%fused_computation.3 | loop fusion | flops 2682880 | bytes 8110080 | tf_op jit(solution)/shard_map/concatenate | solution.py:46
  28.2 4.9 %collective-permute-start.2 = (f32[40,134,3]{1,0,2:T(8,128)S(1)}, f32[40,134,3]{1,0,2:T(8,128)S(1)}, u32[]{:S(2)}, u32[]{:S(2)}) collective-permute-start(f32[40,134,3]{1,0,2:T(8,128)S(1)} %get-tuple-element.20), channel_id=1, source_target_pairs={{0,1},{1,2},{2,3},{4,5},{5,6},{6,7},{8,9},{9,10},{10,11},{12,13},{... | collective-permute-start | bytes 192968 | tf_op jit(solution)/shard_map/ppermute | solution.py:44
  34.8 25.3 %multiply_add_fusion = f32[38,129,128]{1,0,2:T(8,128)} fusion(f32[40,131,128]{1,0,2:T(8,128)S(1)} %get-tuple-element.23, f32[40,131,128]{1,0,2:T(8,128)S(1)} %get-tuple-element.22, f32[129,128]{0,1:T(8,128)S(1)} %get-tuple-element.28, f32[129,128]{0,1:T(8,128)S(1)} %get-tuple-element.29), kind=kLoop, calls=%fused_computation.5 | loop fusion | flops 77177088 | bytes 17700864 | tf_op jit(solution)/shard_map/add | solution.py:86
  60.5 7.2 %maximum_maximum_fusion = (f32[40,134,131]{1,0,2:T(8,128)S(1)}, f32[40,134,131]{1,0,2:T(8,128)S(1)}) fusion(f32[40,3,128]{1,0,2:T(8,128)S(1)} %copy-done.1, f32[2,128,128]{1,0,2:T(2,128)S(1)} %copy.64, f32[38,128,128]{1,0,2:T(8,128)S(1)} %copy.75, f32[40,3,128]{1,0,2:T(8,128)S(1)} %copy-done.2, f32[40,134,3]{1,0,2:T(8,128)S(1)} %collective-permute-done.2, ...), kind=kLoop, calls=%fused_computation.1 | loop fusion | flops 5617280 | bytes 8490240 | tf_op jit(solution)/shard_map/concatenate | solution.py:46
  67.7 13.0 %multiply_add_fusion.3 = f32[38,128,129]{1,0,2:T(8,128)S(1)} fusion(f32[40,134,131]{1,0,2:T(8,128)S(1)} %get-tuple-element.19, f32[40,134,131]{1,0,2:T(8,128)S(1)} %get-tuple-element.18, f32[128,129]{0,1:T(8,128)S(1)} %get-tuple-element.26, f32[128,129]{0,1:T(8,128)S(1)} %get-tuple-element.27), kind=kLoop, calls=%fused_computation.31 | loop fusion | flops 77177088 | bytes 17700864 | tf_op jit(solution)/shard_map/add | solution.py:86
  80.7 4.3 %fusion.44 = f32[38,128,128]{1,0,2:T(8,128)S(1)} fusion(f32[38,128,128]{1,0,2:T(8,128)S(1)} %copy.75, f32[38,128,129]{1,0,2:T(8,128)S(1)} %multiply_add_fusion.3, f32[38,129,128]{1,0,2:T(8,128)} %multiply_add_fusion), kind=kLoop, calls=%fused_computation.60 | loop fusion | flops 3112960 | bytes 14942208 | tf_op jit(solution)/shard_map/sub | solution.py:98
  85.0 2.4 %fusion.78 = f32[128,128,38]{0,2,1:T(8,128)S(1)} fusion(f32[38,128,128]{1,0,2:T(8,128)S(1)} %fusion.44, f32[38,38]{1,0:T(8,128)S(1)} %copy-done), kind=kOutput, calls=%fused_computation.113 | convolution fusion | flops 283901952 | bytes 4986512 | tf_op jit(solution)/shard_map/dot_general | solution.py:110
  87.5 4.1 %bitcast_subtract_fusion.4 = f32[38,128,128]{1,0,2:T(8,128)S(1)} fusion(f32[38,128,128]{1,0,2:T(8,128)S(1)} %fusion.44, f32[128,128,38]{0,2,1:T(8,128)S(1)} %fusion.78, f32[128,128]{0,1:T(8,128)S(1)} %copy.76, f32[38,38]{1,0:T(8,128)S(1)} %copy-done.5), kind=kOutput, calls=%fused_computation.73 | convolution fusion | flops 290127872 | bytes 7542416 | tf_op jit(solution)/shard_map/dot_general | solution.py:117
  91.6 2.5 %fusion.76 = f32[128,128,38]{0,2,1:T(8,128)S(1)} fusion(f32[38,128,128]{1,0,2:T(8,128)S(1)} %bitcast_subtract_fusion.4, f32[38,38]{1,0:T(8,128)S(1)} %copy-done), kind=kOutput, calls=%fused_computation.111 | convolution fusion | flops 283901952 | bytes 4986512 | tf_op jit(solution)/shard_map/dot_general | solution.py:110
  94.1 4.6 %bitcast_subtract_fusion.2 = f32[38,128,128]{1,0,2:T(8,128)S(1)} fusion(f32[38,128,128]{1,0,2:T(8,128)S(1)} %bitcast_subtract_fusion.4, f32[128,128,38]{0,2,1:T(8,128)S(1)} %fusion.76, f32[38,128,128]{1,0,2:T(8,128)S(1)} %fusion.44, f32[128,128]{0,1:T(8,128)S(1)} %copy.76, f32[38,38]{1,0:T(8,128)S(1)} %copy-done.5), kind=kOutput, calls=%fused_computation.69 | convolution fusion | flops 290127872 | bytes 10032784 | tf_op jit(solution)/shard_map/dot_general | solution.py:117
  98.7 2.4 %fusion.74 = f32[128,128,38]{0,2,1:T(8,128)S(1)} fusion(f32[38,128,128]{1,0,2:T(8,128)S(1)} %bitcast_subtract_fusion.2, f32[38,38]{1,0:T(8,128)S(1)} %copy-done), kind=kOutput, calls=%fused_computation.109 | convolution fusion | flops 283901952 | bytes 4986512 | tf_op jit(solution)/shard_map/dot_general | solution.py:110
  101.1 4.4 %fusion.45 = f32[38,128,128]{1,0,2:T(8,128)S(1)} fusion(f32[38,128,128]{1,0,2:T(8,128)S(1)} %fusion.44, f32[38,128,128]{1,0,2:T(8,128)S(1)} %bitcast_subtract_fusion.2, f32[128,128,38]{0,2,1:T(8,128)S(1)} %fusion.74, f32[128,128]{0,1:T(8,128)S(1)} %copy.76, pred[128]{0:T(512)(128)(4,1)S(1)} %gt.22, f32[38,38]{1,0:T(8,128)S(1)} %copy-done.5), kind=kOutput, calls=%fused_computation.65 | convolution fusion | flops 290750464 | bytes 10032912 | tf_op jit(solution)/shard_map/dot_general | solution.py:117
  107.5 13.0 %psum.7 = f32[4,128]{1,0:T(4,128)S(1)} all-reduce(f32[4,128]{1,0:T(4,128)S(1)} %broadcast_multiply_fusion), channel_id=1, replica_groups=mesh['axial'=8,'radial'=4] {'radial'}, use_global_device_ids=true, to_apply=%region_0.1 | all-reduce | flops 512 | bytes 4096 | tf_op jit(solution)/shard_map/psum | solution.py:162
  120.6 2.6 %collective-permute-start.5 = (f32[4,128]{1,0:T(4,128)S(1)}, f32[4,128]{1,0:T(4,128)S(1)}, u32[]{:S(2)}, u32[]{:S(2)}) collective-permute-start(f32[4,128]{1,0:T(4,128)S(1)} %psum.7), channel_id=1, source_target_pairs={{0,28},{4,0},{8,4},{12,8},{16,12},{20,16},{24,20},{28,24},{1,29},{... | collective-permute-start | bytes 6152 | tf_op jit(solution)/shard_map/ppermute | solution.py:30
  123.2 3.3 %copy.77 = f32[38,128,128]{2,1,0:T(8,128)} copy(f32[38,128,128]{1,0,2:T(8,128)} %copy-done.3) | data formatting | bytes 4980736
  126.6 2.6 %collective-permute-start.7 = (f32[4,128]{1,0:T(4,128)S(1)}, f32[4,128]{1,0:T(4,128)S(1)}, u32[]{:S(2)}, u32[]{:S(2)}) collective-permute-start(f32[4,128]{1,0:T(4,128)S(1)} %collective-permute-done.5), channel_id=1, source_target_pairs={{0,28},{4,0},{8,4},{12,8},{16,12},{20,16},{24,20},{28,24},{1,29},{... | collective-permute-start | bytes 6152 | tf_op jit(solution)/shard_map/ppermute | solution.py:30
  130.5 2.6 %collective-permute-start.9 = (f32[4,128]{1,0:T(4,128)S(1)}, f32[4,128]{1,0:T(4,128)S(1)}, u32[]{:S(2)}, u32[]{:S(2)}) collective-permute-start(f32[4,128]{1,0:T(4,128)S(1)} %collective-permute-done.7), channel_id=1, source_target_pairs={{0,28},{4,0},{8,4},{12,8},{16,12},{20,16},{24,20},{28,24},{1,29},{... | collective-permute-start | bytes 6152 | tf_op jit(solution)/shard_map/ppermute | solution.py:30
  134.4 3.9 %collective-permute-done.10 = f32[4,128]{1,0:T(4,128)S(1)} collective-permute-done((f32[4,128]{1,0:T(4,128)S(1)}, f32[4,128]{1,0:T(4,128)S(1)}, u32[]{:S(2)}, u32[]{:S(2)}) %collective-permute-start.10) | collective-permute-done | bytes 2080 | tf_op jit(solution)/shard_map/ppermute | solution.py:25
  138.3 35.0 %gather_fusion = f32[4096]{0:T(1024)S(1)} fusion(f32[4,1024]{1,0:T(4,128)S(1)} %constant_dynamic-update-slice_fusion, s32[4096]{0:T(1024)S(1)} %bitcast.92), kind=kCustom, calls=%fused_computation | custom fusion | bytes 65536 | tf_op jit(solution)/shard_map/jit(take_along_axis)/gather | solution.py:169
  (69 shorter events, 18.6 us)
Async XLA Ops:
  0.6 84.4 %copy-start = (f32[38,38]{1,0:T(8,128)S(1)}, f32[38,38]{1,0:T(8,128)}, u32[]{:S(2)}) copy-start(f32[38,38]{1,0:T(8,128)} %param.13) | copy-start | bytes 17332
  0.6 2.6 %copy-start.4 = (f32[2,128,128]{2,1,0:T(8,128)S(1)}, f32[2,128,128]{2,1,0:T(8,128)}, u32[]{:S(2)}) copy-start(f32[2,128,128]{2,1,0:T(8,128)} %param.11) | copy-start | bytes 393220
  6.7 9.5 %copy-start.6 = (f32[128,128]{1,0:T(8,128)S(1)}, f32[128,128]{1,0:T(8,128)}, u32[]{:S(2)}) copy-start(f32[128,128]{1,0:T(8,128)} %param.12) | copy-start | bytes 196612
  6.7 9.7 %copy-start.10 = (s32[64,1]{0,1:T(1,128)S(1)}, s32[64,1]{0,1:T(1,128)}, u32[]{:S(2)}) copy-start(s32[64,1]{0,1:T(1,128)} %param.15) | copy-start | bytes 772
  9.3 8.2 %collective-permute-start.1 = (f32[40,3,128]{2,0,1:T(8,128)S(1)}, f32[40,3,128]{2,0,1:T(8,128)S(1)}, u32[]{:S(2)}, u32[]{:S(2)}) collective-permute-start(f32[40,3,128]{2,0,1:T(8,128)S(1)} %copy.67), channel_id=1, source_target_pairs={{4,0},{8,4},{12,8},{16,12},{20,16},{24,20},{28,24},{5,1},{9,5},{13... | collective-permute-start | bytes 184328 | tf_op jit(solution)/shard_map/ppermute | solution.py:45
  13.1 6.7 %collective-permute-start = (f32[40,3,128]{2,0,1:T(8,128)S(1)}, f32[40,3,128]{2,0,1:T(8,128)S(1)}, u32[]{:S(2)}, u32[]{:S(2)}) collective-permute-start(f32[40,3,128]{2,0,1:T(8,128)S(1)} %copy.65), channel_id=1, source_target_pairs={{0,4},{4,8},{8,12},{12,16},{16,20},{20,24},{24,28},{1,5},{5,9},{9,... | collective-permute-start | bytes 184328 | tf_op jit(solution)/shard_map/ppermute | solution.py:44
  22.1 1.9 %copy-start.1 = (f32[40,3,128]{1,0,2:T(8,128)S(1)}, f32[40,3,128]{1,0,2:T(8,128)}, u32[]{:S(2)}) copy-start(f32[40,3,128]{1,0,2:T(8,128)} %copy.68) | copy-start | bytes 184324
  22.1 2.6 %copy-start.2 = (f32[40,3,128]{1,0,2:T(8,128)S(1)}, f32[40,3,128]{1,0,2:T(8,128)}, u32[]{:S(2)}) copy-start(f32[40,3,128]{1,0,2:T(8,128)} %copy.66) | copy-start | bytes 184324
  28.2 31.9 %collective-permute-start.2 = (f32[40,134,3]{1,0,2:T(8,128)S(1)}, f32[40,134,3]{1,0,2:T(8,128)S(1)}, u32[]{:S(2)}, u32[]{:S(2)}) collective-permute-start(f32[40,134,3]{1,0,2:T(8,128)S(1)} %get-tuple-element.20), channel_id=1, source_target_pairs={{0,1},{1,2},{2,3},{4,5},{5,6},{6,7},{8,9},{9,10},{10,11},{12,13},{... | collective-permute-start | bytes 192968 | tf_op jit(solution)/shard_map/ppermute | solution.py:44
  33.1 26.9 %collective-permute-start.3 = (f32[40,134,3]{1,0,2:T(8,128)S(1)}, f32[40,134,3]{1,0,2:T(8,128)S(1)}, u32[]{:S(2)}, u32[]{:S(2)}) collective-permute-start(f32[40,134,3]{1,0,2:T(8,128)S(1)} %get-tuple-element.21), channel_id=1, source_target_pairs={{1,0},{2,1},{3,2},{5,4},{6,5},{7,6},{9,8},{10,9},{11,10},{13,12},{... | collective-permute-start | bytes 192968 | tf_op jit(solution)/shard_map/ppermute | solution.py:45
  85.0 2.5 %copy-start.5 = (f32[38,38]{1,0:T(8,128)S(1)}, f32[38,38]{1,0:T(8,128)}, u32[]{:S(2)}) copy-start(f32[38,38]{1,0:T(8,128)} %param.14) | copy-start | bytes 17332
  101.1 4.4 %copy-start.8 = (f32[4,38]{1,0:T(4,128)S(1)}, f32[4,38]{1,0:T(4,128)}, u32[]{:S(2)}) copy-start(f32[4,38]{1,0:T(4,128)} %param.16) | copy-start | bytes 1828
  105.5 15.1 %copy-start.3 = (f32[38,128,128]{1,0,2:T(8,128)}, f32[38,128,128]{1,0,2:T(8,128)S(1)}, u32[]{:S(2)}) copy-start(f32[38,128,128]{1,0,2:T(8,128)S(1)} %fusion.45) | copy-start | bytes 7471108
  105.5 1.7 copy-start.9
  120.5 6.0 %collective-permute-start.4 = (f32[4,128]{1,0:T(4,128)S(1)}, f32[4,128]{1,0:T(4,128)S(1)}, u32[]{:S(2)}, u32[]{:S(2)}) collective-permute-start(f32[4,128]{1,0:T(4,128)S(1)} %psum.7), channel_id=1, source_target_pairs={{0,4},{4,8},{8,12},{12,16},{16,20},{20,24},{24,28},{28,0},{1,5},{5... | collective-permute-start | bytes 6152 | tf_op jit(solution)/shard_map/ppermute | solution.py:25
  120.6 6.0 %collective-permute-start.5 = (f32[4,128]{1,0:T(4,128)S(1)}, f32[4,128]{1,0:T(4,128)S(1)}, u32[]{:S(2)}, u32[]{:S(2)}) collective-permute-start(f32[4,128]{1,0:T(4,128)S(1)} %psum.7), channel_id=1, source_target_pairs={{0,28},{4,0},{8,4},{12,8},{16,12},{20,16},{24,20},{28,24},{1,29},{... | collective-permute-start | bytes 6152 | tf_op jit(solution)/shard_map/ppermute | solution.py:30
  126.5 3.9 %collective-permute-start.6 = (f32[4,128]{1,0:T(4,128)S(1)}, f32[4,128]{1,0:T(4,128)S(1)}, u32[]{:S(2)}, u32[]{:S(2)}) collective-permute-start(f32[4,128]{1,0:T(4,128)S(1)} %collective-permute-done.4), channel_id=1, source_target_pairs={{0,4},{4,8},{8,12},{12,16},{16,20},{20,24},{24,28},{28,0},{1,5},{5... | collective-permute-start | bytes 6152 | tf_op jit(solution)/shard_map/ppermute | solution.py:25
  126.6 4.0 %collective-permute-start.7 = (f32[4,128]{1,0:T(4,128)S(1)}, f32[4,128]{1,0:T(4,128)S(1)}, u32[]{:S(2)}, u32[]{:S(2)}) collective-permute-start(f32[4,128]{1,0:T(4,128)S(1)} %collective-permute-done.5), channel_id=1, source_target_pairs={{0,28},{4,0},{8,4},{12,8},{16,12},{20,16},{24,20},{28,24},{1,29},{... | collective-permute-start | bytes 6152 | tf_op jit(solution)/shard_map/ppermute | solution.py:30
  130.5 3.9 %collective-permute-start.8 = (f32[4,128]{1,0:T(4,128)S(1)}, f32[4,128]{1,0:T(4,128)S(1)}, u32[]{:S(2)}, u32[]{:S(2)}) collective-permute-start(f32[4,128]{1,0:T(4,128)S(1)} %collective-permute-done.6), channel_id=1, source_target_pairs={{0,4},{4,8},{8,12},{12,16},{16,20},{20,24},{24,28},{28,0},{1,5},{5... | collective-permute-start | bytes 6152 | tf_op jit(solution)/shard_map/ppermute | solution.py:25
  130.5 3.9 %collective-permute-start.9 = (f32[4,128]{1,0:T(4,128)S(1)}, f32[4,128]{1,0:T(4,128)S(1)}, u32[]{:S(2)}, u32[]{:S(2)}) collective-permute-start(f32[4,128]{1,0:T(4,128)S(1)} %collective-permute-done.7), channel_id=1, source_target_pairs={{0,28},{4,0},{8,4},{12,8},{16,12},{20,16},{24,20},{28,24},{1,29},{... | collective-permute-start | bytes 6152 | tf_op jit(solution)/shard_map/ppermute | solution.py:30
  134.4 3.9 %collective-permute-start.10 = (f32[4,128]{1,0:T(4,128)S(1)}, f32[4,128]{1,0:T(4,128)S(1)}, u32[]{:S(2)}, u32[]{:S(2)}) collective-permute-start(f32[4,128]{1,0:T(4,128)S(1)} %collective-permute-done.8), channel_id=1, source_target_pairs={{0,4},{4,8},{8,12},{12,16},{16,20},{20,24},{24,28},{28,0},{1,5},{5... | collective-permute-start | bytes 6152 | tf_op jit(solution)/shard_map/ppermute | solution.py:25
  138.3 35.0 %copy-start.7 = (f32[4,1024]{1,0:T(4,128)S(1)}, f32[4,1024]{1,0:T(4,128)}, u32[]{:S(2)}) copy-start(f32[4,1024]{1,0:T(4,128)} %param.19) | copy-start | bytes 49156
